TPU v7x, 256 devices: a whole 4x4x8 slice. The times are simulated.
256 devices in a mesh: dp: 64 (over y, z, core), seq: 4 (over x).
Axes of the slice: x: 4, y: 4, z: 8, core: 2. Of those that a mesh axis runs over, the one named last changes fastest.
Arguments:
- frames: bfloat16 [32768, 1536], P('dp', 'seq')
- owner_slot: int32 [32768], P('dp'), may hold values from -1 to 32767, as said below
- segment: int32 [64, 512], P('dp'), may hold values from 0 to 2, never falling along the last dimension, each value on 1 to 256 neighbouring positions
- norm_gain: float32 [1536], replicated, may hold values from 0.25 to 1.75
- expand: bfloat16 [1536, 2, 1536], P('dp', None, 'seq'), may hold values from -0.15625 to 0.15625
- kernel: float32 [9, 1536], P(None, 'seq'), may hold values from -2.5 to 2.5
- project: bfloat16 [1536, 1536], P('seq', 'dp'), may hold values from -0.15625 to 0.15625
- cotangent: bfloat16 [32768, 1536], P('dp', 'seq'), may hold values from -6 to 6
Outputs:
- output: bfloat16 [32768, 1536], P('dp', 'seq')
- grad_frames: bfloat16 [32768, 1536], P('dp', 'seq')
- grad_gain: float32 [1536], P('seq')
- grad_kernel: float32 [9, 1536], P(None, 'seq')
- grad_expand: float32 [1536, 2, 1536], P('dp', None, 'seq')
- grad_project: float32 [1536, 1536], P('seq', 'dp')
Inputs may be any that keep to these rules, and one draw needn't show every extreme that they name: `owner_slot`: for each arrival row, the balanced row that takes it, or -1 for an empty arrival row; no balanced row is named twice. The live rows of each pack come first, contiguous, ordered by sending index of dp and then by arrival row; empty rows fill the pack's tail. Of the 512 arrival rows of one index of dp, at most 8 name rows of any one pack; some pack takes exactly 8 rows from every index of dp. `segment`: within each pack the utterance numbers never fall; a pack holds 3 utterances of 1 to 256 frames, one of exactly 256.
All inputs are finite; a program needn't handle non-finite values.
Results may differ from a plain program's by a relative error of at most 0.01.
Values may be sent and summed in bfloat16 or wider, within the bound.
No kernel may reach another device: no remote copies, remote signals or barrier semaphores. Data moves between devices by JAX's collectives and lax.ppermute only.
A program may use at most 128 MiB of HBM per device.

v0:
```python
import math
import jax
import jax.numpy as jnp
from jax import lax
from jax.sharding import PartitionSpec as P

D = 1536
KSIZE = 9
EPS = 1e-05


def conv_masks(labels):
    half_width = (KSIZE - 1) // 2
    length = labels.shape[0]
    padded = jnp.pad(labels, (half_width, half_width), constant_values=-1)
    return [
        (padded[tap_index : tap_index + length] == labels).astype(jnp.float32)[:, None]
        for tap_index in range(KSIZE)
    ]


def depthwise(signal, kernel, tap_masks):
    half_width = (KSIZE - 1) // 2
    length = signal.shape[0]
    padded = jnp.pad(signal, ((half_width, half_width), (0, 0)))
    total = jnp.zeros(signal.shape, jnp.float32)
    for tap_index in range(KSIZE):
        total = (
            total
            + kernel[tap_index] * padded[tap_index : tap_index + length] * tap_masks[tap_index]
        )
    return total


def depthwise_back(signal, upstream, kernel, tap_masks):
    half_width = (KSIZE - 1) // 2
    length = signal.shape[0]
    padded = jnp.pad(signal, ((half_width, half_width), (0, 0)))
    spread = jnp.zeros((length + 2 * half_width, signal.shape[1]), jnp.float32)
    tap_sums = []
    for tap_index in range(KSIZE):
        masked = upstream * tap_masks[tap_index]
        tap_sums.append(jnp.sum(masked * padded[tap_index : tap_index + length], axis=0))
        spread = spread + jnp.pad(
            kernel[tap_index] * masked, ((tap_index, 2 * half_width - tap_index), (0, 0))
        )
    return (jnp.stack(tap_sums), spread[half_width : half_width + length])


def place_rows(incoming, landing, row_count):
    flat = incoming.reshape(-1, incoming.shape[-1])
    total_slots = flat.shape[0]
    inverse = (
        jnp.full((row_count + 1,), total_slots, jnp.int32)
        .at[landing.reshape(-1)]
        .set(jnp.arange(total_slots, dtype=jnp.int32))[:row_count]
    )
    padded = jnp.concatenate([flat, jnp.zeros((1, flat.shape[1]), flat.dtype)])
    return (padded[inverse], inverse < total_slots)


def shards(frames, owner_slot, segment, norm_gain, expand, kernel, project, cotangent):
    row_count, quarter = frames.shape
    groups = lax.axis_size("dp")
    lane_index = lax.axis_index("seq")
    capacity = row_count // groups
    bucket_slots = groups * capacity
    dest_group = jnp.where(owner_slot >= 0, owner_slot // row_count, groups)
    onehot = (dest_group[:, None] == jnp.arange(groups, dtype=jnp.int32)[None, :]).astype(jnp.int32)
    earlier = jnp.cumsum(onehot, axis=0) - onehot
    within = jnp.sum(earlier * onehot, axis=1)
    send_pos = jnp.where(owner_slot >= 0, dest_group * capacity + within, bucket_slots)
    source_row = (
        jnp.full((bucket_slots + 1,), row_count, jnp.int32)
        .at[send_pos]
        .set(jnp.arange(row_count, dtype=jnp.int32))[:bucket_slots]
    )
    slot_padded = jnp.concatenate([owner_slot, jnp.full((1,), -1, jnp.int32)])
    named_slot = slot_padded[source_row]
    landing_out = jnp.where(named_slot >= 0, named_slot % row_count, row_count).reshape(
        groups, capacity
    )
    padded_in = jnp.concatenate([frames, jnp.zeros((1, quarter), jnp.bfloat16)])
    outgoing = padded_in[source_row].reshape(groups, capacity, quarter)
    incoming, landing = (
        lax.all_to_all(outgoing, "dp", split_axis=0, concat_axis=0, tiled=True),
        lax.all_to_all(landing_out, "dp", split_axis=0, concat_axis=0, tiled=True),
    )
    local_rows, occupied = place_rows(incoming, landing, row_count)
    whole_rows = lax.all_gather(local_rows, "seq", axis=1, tiled=True)
    live_col = occupied.astype(jnp.float32)[:, None]
    floats = whole_rows.astype(jnp.float32)
    row_mean = jnp.mean(floats, axis=1, keepdims=True)
    centred = floats - row_mean
    inv_scale = lax.rsqrt(jnp.mean(centred * centred, axis=1, keepdims=True) + EPS)
    normed = centred * inv_scale
    scaled = (normed * norm_gain).astype(jnp.bfloat16)
    expand_full = lax.all_gather(expand, "dp", axis=0, tiled=True).reshape(D, 2 * quarter)
    project_full = lax.all_gather(project, "dp", axis=1, tiled=True)
    joined = jnp.dot(scaled, expand_full, preferred_element_type=jnp.float32)
    value_half = joined[:, :quarter]
    gate_sig = jax.nn.sigmoid(joined[:, quarter:])
    glu_out = value_half * gate_sig
    tap_masks = conv_masks(segment[0])
    conv_out = depthwise(glu_out, kernel, tap_masks)
    conv_sig = jax.nn.sigmoid(conv_out)
    hidden = (conv_out * conv_sig * live_col).astype(jnp.bfloat16)
    partial_out = jnp.dot(hidden, project_full, preferred_element_type=jnp.float32)
    mixed_share = lax.psum_scatter(
        partial_out.astype(jnp.bfloat16), "seq", scatter_dimension=1, tiled=True
    ).astype(jnp.float32)
    output = (local_rows.astype(jnp.float32) + mixed_share).astype(jnp.bfloat16)
    inv_root = 1.0 / math.sqrt(row_count * groups)
    cot_full = lax.all_gather(cotangent, "seq", axis=1, tiled=True)
    project_term = lax.dot_general(
        hidden, cot_full, (((0,), (0,)), ((), ())), preferred_element_type=jnp.float32
    )
    grad_project = lax.psum_scatter(project_term, "dp", scatter_dimension=1, tiled=True) * inv_root
    hidden_grad = (
        lax.dot_general(
            cot_full, project_full, (((1,), (1,)), ((), ())), preferred_element_type=jnp.float32
        )
        * live_col
    )
    conv_grad = hidden_grad * (conv_sig + conv_out * conv_sig * (1.0 - conv_sig))
    kernel_term, glu_grad = depthwise_back(glu_out, conv_grad, kernel, tap_masks)
    proj_grad = jnp.concatenate(
        [glu_grad * gate_sig, glu_grad * value_half * gate_sig * (1.0 - gate_sig)], axis=1
    ).astype(jnp.bfloat16)
    term_block = lax.dot_general(
        scaled, proj_grad, (((0,), (0,)), ((), ())), preferred_element_type=jnp.float32
    )
    grad_expand = (
        lax.psum_scatter(
            term_block.reshape(expand.shape[0] * lax.axis_size("dp"), 2, quarter),
            "dp",
            scatter_dimension=0,
            tiled=True,
        )
        * inv_root
    )
    scaled_part = lax.dot_general(
        proj_grad, expand_full, (((1,), (1,)), ((), ())), preferred_element_type=jnp.float32
    )
    normed_local = lax.dynamic_slice_in_dim(normed, lane_index * quarter, quarter, 1)
    scaled_grad = lax.psum(scaled_part.astype(jnp.bfloat16), "seq").astype(jnp.float32)
    normed_grad = scaled_grad * norm_gain
    first_mean = jnp.mean(normed_grad, axis=1, keepdims=True)
    second_mean = jnp.mean(normed_grad * normed, axis=1, keepdims=True)
    full_grad = inv_scale * (normed_grad - first_mean - normed * second_mean)
    packed_grad = lax.dynamic_slice_in_dim(full_grad, lane_index * quarter, quarter, 1)
    scaled_share = lax.dynamic_slice_in_dim(scaled_grad, lane_index * quarter, quarter, 1)
    gain_term = jnp.sum(scaled_share * normed_local, axis=0)
    gain_sum, kernel_sum = lax.psum((gain_term, kernel_term), "dp")
    back_rows = (packed_grad + cotangent.astype(jnp.float32)).astype(jnp.bfloat16)
    back_padded = jnp.concatenate([back_rows, jnp.zeros((1, quarter), jnp.bfloat16)])
    returning = back_padded[landing.reshape(-1)].reshape(groups, capacity, quarter)
    returned = lax.all_to_all(returning, "dp", split_axis=0, concat_axis=0, tiled=True)
    returned_flat = jnp.concatenate(
        [returned.reshape(bucket_slots, quarter), jnp.zeros((1, quarter), jnp.bfloat16)]
    )
    grad_frames = returned_flat[send_pos]
    return (
        output,
        grad_frames,
        gain_sum * inv_root,
        kernel_sum * inv_root,
        grad_expand,
        grad_project,
    )


def solution(mesh):
    placed = (
        P("dp", "seq"),
        P("dp"),
        P("dp", None),
        P(),
        P("dp", None, "seq"),
        P(None, "seq"),
        P("seq", "dp"),
        P("dp", "seq"),
    )
    return jax.shard_map(
        shards,
        mesh=mesh,
        in_specs=placed,
        out_specs=(
            P("dp", "seq"),
            P("dp", "seq"),
            P("seq"),
            P(None, "seq"),
            P("dp", None, "seq"),
            P("seq", "dp"),
        ),
        check_vma=False,
    )
```

profile of v0, /device:TPU:4, one launch (start us, length us, event | category | flops | bytes accessed | tf_op | source)
XLA Modules:
  0.0 722.8 jit_solution(6718990988851698500)
XLA Ops:
  10.9 2.4 scatter_custom_fusion
  17.1 12.1 %all-to-all-start.1 = ((s32[64,1,8]{2,1,0:T(1,128)}), s32[64,1,8]{2,1,0:T(1,128)S(1)}, u32[]{:S(2)}, u32[]{:S(2)}) async-start(s32[64,1,8]{2,1,0:T(1,128)} %bitcast.4), calls=%async_computation.1 | async-start | bytes 65536 | tf_op jit(solution)/shard_map/all_to_all | solution.py:87
  29.3 2.6 gather_fusion
  31.9 6.8 all-to-all-done.1
  38.7 4.6 all-to-all-start
  44.8 2.4 scatter_custom_fusion.1
  47.2 10.6 %all-to-all-done = bf16[64,8,384]{2,1,0:T(8,128)(2,1)S(1)} async-done(((bf16[64,8,384]{2,1,0:T(8,128)(2,1)}), bf16[64,8,384]{2,1,0:T(8,128)(2,1)S(1)}, u32[]{:S(2)}, u32[]{:S(2)}) %all-to-all-start) | async-done | bytes 393248 | tf_op jit(solution)/shard_map/all_to_all | solution.py:86
  57.9 2.6 gather_fusion.2
  63.0 22.6 %all-gather.12.cloned.1.call-done = bf16[512,1536]{1,0:T(8,128)(2,1)} async-done(((bf16[512,384]{1,0:T(8,128)(2,1)}), bf16[512,1536]{1,0:T(8,128)(2,1)}) %all-gather.12.cloned.1.call-update) | async-done | bytes 1572880 | tf_op jit(solution)/shard_map/all_gather | solution.py:90
  88.0 79.3 %all-gather.6.cloned.1.call-done = bf16[1536,2,384]{2,1,0:T(2,128)(2,1)} async-done(((bf16[24,2,384]{2,1,0:T(2,128)(2,1)}), bf16[1536,2,384]{2,1,0:T(2,128)(2,1)}) %all-gather.6.cloned.1.call-update) | async-done | bytes 2359312 | tf_op jit(solution)/shard_map/all_gather | solution.py:98
  174.1 70.2 %all-gather.8.cloned.1.call-done = bf16[384,1536]{0,1:T(8,128)(2,1)} async-done(((bf16[384,24]{0,1:T(8,128)(2,1)}), bf16[384,1536]{0,1:T(8,128)(2,1)}) %all-gather.8.cloned.1.call-update) | async-done | bytes 1179664 | tf_op jit(solution)/shard_map/all_gather | solution.py:99
  244.4 27.2 %all-gather.10.cloned.1.call-done = bf16[512,1536]{1,0:T(8,128)(2,1)} async-done(((bf16[512,384]{1,0:T(8,128)(2,1)}), bf16[512,1536]{1,0:T(8,128)(2,1)}) %all-gather.10.cloned.1.call-update) | async-done | bytes 1572880 | tf_op jit(solution)/shard_map/all_gather | solution.py:114
  271.6 7.9 %multiply_reduce_fusion.1 = (f32[384]{0:T(512)}, f32[384]{0:T(512)}, f32[384]{0:T(512)}, f32[384]{0:T(512)}, f32[384]{0:T(512)}, /*index=5*/f32[384]{0:T(512)}, ...) fusion(f32[512,384]{1,0:T(8,128)} %copy-done.3, ...), kind=kOutput, calls=%fused_computation.36 | convolution fusion | flops 611054208 | bytes 5932032 | tf_op jit(solution)/shard_map/dot_general | solution.py:120
  282.8 2.6 convolution_convert_fusion
  285.5 4.8 fusion.12
  290.3 8.2 %copy.19 = f32[1536,2,384]{2,1,0:T(2,128)} copy(f32[1536,2,384]{0,2,1:T(8,128)} %bitcast.41) | data formatting | bytes 9437184 | tf_op jit(solution)/shard_map/reshape | solution.py:135
  299.1 2.6 convolution_convert_fusion.1
  303.5 4.2 fusion.46
  308.4 32.9 %all-reduce.21.cloned.1.call-done = bf16[512,1536]{1,0:T(8,128)(2,1)} async-done(((bf16[512,1536]{1,0:T(8,128)(2,1)}), bf16[512,1536]{1,0:T(8,128)(2,1)}) %all-reduce.21.cloned.1.call-update) | async-done | bytes 1572880 | tf_op jit(solution)/shard_map/psum | solution.py:146
  344.8 2.6 gather_fusion.3
  347.4 10.5 %all-to-all-start.2 = ((bf16[64,8,384]{2,1,0:T(8,128)(2,1)}), bf16[64,8,384]{2,1,0:T(8,128)(2,1)S(1)}, u32[]{:S(2)}, u32[]{:S(2)}) async-start(bf16[64,8,384]{2,1,0:T(8,128)(2,1)} %bitcast.7), calls=%async_computation.2 | async-start | bytes 786432 | tf_op jit(solution)/shard_map/all_to_all | solution.py:158
  359.4 251.8 %all-reduce.17 = (f32[384]{0:T(512)S(1)}, f32[9,384]{1,0:T(8,128)S(1)}) all-reduce(f32[384]{0:T(512)S(1)} %get-tuple-element.30, f32[9,384]{1,0:T(8,128)S(1)} %stack.39), channel_id=1, replica_groups=mesh['dp'=64,'seq'=4] {'dp'}, use_global_device_ids=true, to_apply=%region_12.13 | all-reduce | flops 3840 | bytes 30720 | tf_op jit(solution)/shard_map/psum | solution.py:154
  612.4 2.6 gather_fusion.4
  618.6 95.9 %reduce-scatter.9.cloned.1.call-done = f32[384,24]{0,1:T(8,128)} async-done(((f32[384,1536]{0,1:T(8,128)}), f32[384,24]{0,1:T(8,128)}) %reduce-scatter.9.cloned.1.call-update) | async-done | bytes 36880
  (141 shorter events, 37.4 us)
Async XLA Ops:
  7.2 22.1 %copy-start.7 = (bf16[512,384]{1,0:T(8,128)(2,1)S(1)}, bf16[512,384]{1,0:T(8,128)(2,1)}, u32[]{:S(2)}) copy-start(bf16[512,384]{1,0:T(8,128)(2,1)} %param.8) | copy-start | bytes 1179652
  17.1 21.6 %all-to-all-start.1 = ((s32[64,1,8]{2,1,0:T(1,128)}), s32[64,1,8]{2,1,0:T(1,128)S(1)}, u32[]{:S(2)}, u32[]{:S(2)}) async-start(s32[64,1,8]{2,1,0:T(1,128)} %bitcast.4), calls=%async_computation.1 | async-start | bytes 65536 | tf_op jit(solution)/shard_map/all_to_all | solution.py:87
  38.7 19.1 %all-to-all-start = ((bf16[64,8,384]{2,1,0:T(8,128)(2,1)}), bf16[64,8,384]{2,1,0:T(8,128)(2,1)S(1)}, u32[]{:S(2)}, u32[]{:S(2)}) async-start(bf16[64,8,384]{2,1,0:T(8,128)(2,1)} %bitcast.2), calls=%async_computation | async-start | bytes 786432 | tf_op jit(solution)/shard_map/all_to_all | solution.py:86
  43.3 42.2 %all-gather.12.cloned.1.call-start = ((), (), s32[]{:S(2)}) async-start(), calls=%async_computation.9 | async-start | bytes 1966080 | tf_op jit(solution)/shard_map/all_gather | solution.py:90
  60.5 106.8 %all-gather.6.cloned.1.call-start = ((), (), s32[]{:S(2)}) async-start(), calls=%async_computation.5 | async-start | bytes 2396160 | tf_op jit(solution)/shard_map/all_gather | solution.py:98
  61.3 183.1 %all-gather.8.cloned.1.call-start = ((), (), s32[]{:S(2)}) async-start(), calls=%async_computation.6 | async-start | bytes 1198080 | tf_op jit(solution)/shard_map/all_gather | solution.py:99
  62.0 209.6 %all-gather.10.cloned.1.call-start = ((), (), s32[]{:S(2)}) async-start(), calls=%async_computation.7 | async-start | bytes 1966080 | tf_op jit(solution)/shard_map/all_gather | solution.py:114
  62.6 278.7 %all-reduce.21.cloned.1.call-start = ((), (), s32[]{:S(2)}) async-start(), calls=%async_computation.8 | async-start | bytes 3145728 | tf_op jit(solution)/shard_map/psum | solution.py:146
  63.0 208.7 %copy-start.25 = (f32[512]{0:T(512)}, f32[512]{0:T(512)S(1)}, u32[]{:S(2)}) copy-start(f32[512]{0:T(512)S(1)} %compare_convert_fusion) | copy-start | bytes 6148
  285.5 329.6 %all-reduce.23.cloned.1.call-start = ((), (), s32[]{:S(2)}) async-start(), calls=%async_computation.11 | async-start | bytes 9437184
  298.4 318.1 %reduce-scatter.7.cloned.1.call-start = ((), (), s32[]{:S(2)}) async-start(), calls=%async_computation.10 | async-start | bytes 1966080
  303.3 411.3 %reduce-scatter.9.cloned.1.call-start = ((), (), s32[]{:S(2)}) async-start(), calls=%async_computation.12 | async-start | bytes 2396160
  344.7 13.2 %copy-start.27 = (u32[256]{0:T(256)S(1)}, u32[256]{0:T(256)}, u32[]{:S(2)}) copy-start(u32[256]{0:T(256)} %constant.110) | copy-start | bytes 3076
  344.7 14.4 %copy-start.11 = (s32[512]{0:T(512)S(1)}, s32[512]{0:T(512)}, u32[]{:S(2)}) copy-start(s32[512]{0:T(512)} %copy-done.10) | copy-start | bytes 6148
  344.7 14.4 %copy-start.24 = (f32[384]{0:T(512)S(1)}, f32[384]{0:T(512)}, u32[]{:S(2)}) copy-start(f32[384]{0:T(512)} %get-tuple-element.9) | copy-start | bytes 4612
  344.8 14.4 %copy-start.23 = (f32[384]{0:T(512)S(1)}, f32[384]{0:T(512)}, u32[]{:S(2)}) copy-start(f32[384]{0:T(512)} %get-tuple-element.10) | copy-start | bytes 4612
  344.8 14.4 %copy-start.22 = (f32[384]{0:T(512)S(1)}, f32[384]{0:T(512)}, u32[]{:S(2)}) copy-start(f32[384]{0:T(512)} %get-tuple-element.11) | copy-start | bytes 4612
  344.8 14.5 %copy-start.21 = (f32[384]{0:T(512)S(1)}, f32[384]{0:T(512)}, u32[]{:S(2)}) copy-start(f32[384]{0:T(512)} %get-tuple-element.12) | copy-start | bytes 4612
  344.8 14.5 %copy-start.20 = (f32[384]{0:T(512)S(1)}, f32[384]{0:T(512)}, u32[]{:S(2)}) copy-start(f32[384]{0:T(512)} %get-tuple-element.16) | copy-start | bytes 4612
  344.8 14.5 %copy-start.19 = (f32[384]{0:T(512)S(1)}, f32[384]{0:T(512)}, u32[]{:S(2)}) copy-start(f32[384]{0:T(512)} %get-tuple-element.13) | copy-start | bytes 4612
  344.8 14.5 %copy-start.18 = (f32[384]{0:T(512)S(1)}, f32[384]{0:T(512)}, u32[]{:S(2)}) copy-start(f32[384]{0:T(512)} %get-tuple-element.14) | copy-start | bytes 4612
  344.8 14.5 %copy-start.17 = (f32[384]{0:T(512)S(1)}, f32[384]{0:T(512)}, u32[]{:S(2)}) copy-start(f32[384]{0:T(512)} %get-tuple-element.15) | copy-start | bytes 4612
  344.8 14.5 %copy-start.16 = (f32[384]{0:T(512)S(1)}, f32[384]{0:T(512)}, u32[]{:S(2)}) copy-start(f32[384]{0:T(512)} %get-tuple-element.8) | copy-start | bytes 4612
  347.4 265.0 %all-to-all-start.2 = ((bf16[64,8,384]{2,1,0:T(8,128)(2,1)}), bf16[64,8,384]{2,1,0:T(8,128)(2,1)S(1)}, u32[]{:S(2)}, u32[]{:S(2)}) async-start(bf16[64,8,384]{2,1,0:T(8,128)(2,1)} %bitcast.7), calls=%async_computation.2 | async-start | bytes 786432 | tf_op jit(solution)/shard_map/all_to_all | solution.py:158
  (15 other events, 44.9 us)
Sparse Core Ops, SparseCore 0:
  60.6 24.8 all-gather.11
  88.2 79.0 all-gather.5
  170.0 74.3 all-gather.7
  246.1 25.4 all-gather.9
  285.6 55.6 all-reduce.20
  344.7 201.8 all-reduce.22
  549.1 25.4 reduce-scatter.6
  578.7 135.7 reduce-scatter.8
where the time goes:
time: 724 us; the launch traced here: 723 us
  waiting for transfers between devices  348 us (48%)
  blocking collectives  252 us (35%)
  local copies, waits for them, and re-layouts  36.2 us (5%)
  starting transfers between devices  27.9 us (4%)
  matrix products  23.5 us (3%)
  other arithmetic  20.3 us (3%)
  between operations  15.4 us (2%)
    psum x1, blocking collectives, shards(): gain_sum, kernel_sum = lax.psum((gain_term, kernel_term), 'dp')  252 us
    unnamed x11, waiting for transfers between devices  97.9 us
    all_gather x1, waiting for transfers between devices, shards(): lax.all_gather(expand, 'dp', axis=0, tiled=True).reshape(D, 2 * quarter)  79.3 us
    all_gather x1, waiting for transfers between devices, shards(): project_full = lax.all_gather(project, 'dp', axis=1, tiled=True)  70.2 us
    psum x1, waiting for transfers between devices, shards(): lax.psum(scaled_part.astype(jnp.bfloat16), 'seq').astype(jnp.float32)  32.9 us
    all_gather x1, waiting for transfers between devices, shards(): cot_full = lax.all_gather(cotangent, 'seq', axis=1, tiled=True)  27.2 us
    all_gather x1, waiting for transfers between devices, shards(): whole_rows = lax.all_gather(local_rows, 'seq', axis=1, tiled=True)  22.6 us
  transfers between devices with their start and end apart: 11, of which 8 were waited for; matrix products, arithmetic and copies ran while one was open for 7% of the time, Pallas kernels for 0%

commit v1 on v0

--- a/solution.py
+++ b/solution.py
@@ -143,7 +143,9 @@
         proj_grad, expand_full, (((1,), (1,)), ((), ())), preferred_element_type=jnp.float32
     )
     normed_local = lax.dynamic_slice_in_dim(normed, lane_index * quarter, quarter, 1)
-    scaled_grad = lax.psum(scaled_part.astype(jnp.bfloat16), "seq").astype(jnp.float32)
+    scaled_grad = jnp.sum(lax.all_gather(scaled_part.astype(jnp.bfloat16), "seq"), axis=0).astype(
+        jnp.float32
+    )
     normed_grad = scaled_grad * norm_gain
     first_mean = jnp.mean(normed_grad, axis=1, keepdims=True)
     second_mean = jnp.mean(normed_grad * normed, axis=1, keepdims=True)

time: 724 us -> 990 us (1.37)
  waiting for transfers between devices: 348 us -> 615 us
    unnamed x11, waiting for transfers between devices: 97.9 us -> 329 us
    all_gather x0 -> x1, waiting for transfers between devices: none -> 69.5 us  [shards(): lax.all_gather(scaled_part.astype(jnp.bfloat16), 'seq')]
    psum x1 -> x0, waiting for transfers between devices: 32.9 us -> none  [shards(): lax.psum(scaled_part.astype(jnp.bfloat16), 'seq').astype(jnp.float32)]
  transfers between devices with their start and end apart: 11 -> 11, of which waited for: 8 -> 10; matrix products, arithmetic and copies ran while one was open for 7% -> 5% of each run, Pallas kernels for 0% -> 0%
where the time goes in v1:
time: 990 us; the launch traced here: 989 us
  waiting for transfers between devices  615 us (62%)
  blocking collectives  246 us (25%)
  local copies, waits for them, and re-layouts  36.1 us (4%)
  starting transfers between devices  27.9 us (3%)
  matrix products  24.5 us (2%)
  other arithmetic  23.5 us (2%)
  between operations  15.4 us (2%)
    unnamed x11, waiting for transfers between devices  329 us
    psum x1, blocking collectives, shards(): gain_sum, kernel_sum = lax.psum((gain_term, kernel_term), 'dp')  246 us
    all_gather x1, waiting for transfers between devices, shards(): lax.all_gather(expand, 'dp', axis=0, tiled=True).reshape(D, 2 * quarter)  79.3 us
    all_gather x1, waiting for transfers between devices, shards(): project_full = lax.all_gather(project, 'dp', axis=1, tiled=True)  70.2 us
    all_gather x1, waiting for transfers between devices, shards(): lax.all_gather(scaled_part.astype(jnp.bfloat16), 'seq')  69.5 us
    all_gather x1, waiting for transfers between devices, shards(): cot_full = lax.all_gather(cotangent, 'seq', axis=1, tiled=True)  27.2 us
    all_gather x1, waiting for transfers between devices, shards(): whole_rows = lax.all_gather(local_rows, 'seq', axis=1, tiled=True)  22.6 us
  transfers between devices with their start and end apart: 11, of which 10 were waited for; matrix products, arithmetic and copies ran while one was open for 5% of the time, Pallas kernels for 0%

profile of v1, /device:TPU:4, one launch (start us, length us, event | category | flops | bytes accessed | tf_op | source)
XLA Modules:
  0.0 988.8 jit_solution(17328579810417582964)
XLA Ops:
  17.1 12.1 %all-to-all-start.1 = ((s32[64,1,8]{2,1,0:T(1,128)}), s32[64,1,8]{2,1,0:T(1,128)S(1)}, u32[]{:S(2)}, u32[]{:S(2)}) async-start(s32[64,1,8]{2,1,0:T(1,128)} %bitcast.4), calls=%async_computation.1 | async-start | bytes 65536 | tf_op jit(solution)/shard_map/all_to_all | solution.py:87
  29.3 2.6 gather_fusion
  31.9 6.8 all-to-all-done.1
  38.7 4.6 all-to-all-start
  47.2 10.6 %all-to-all-done = bf16[64,8,384]{2,1,0:T(8,128)(2,1)S(1)} async-done(((bf16[64,8,384]{2,1,0:T(8,128)(2,1)}), bf16[64,8,384]{2,1,0:T(8,128)(2,1)S(1)}, u32[]{:S(2)}, u32[]{:S(2)}) %all-to-all-start) | async-done | bytes 393248 | tf_op jit(solution)/shard_map/all_to_all | solution.py:86
  57.9 2.6 gather_fusion.2
  63.0 22.6 %all-gather.14.cloned.1.call-done = bf16[512,1536]{1,0:T(8,128)(2,1)} async-done(((bf16[512,384]{1,0:T(8,128)(2,1)}), bf16[512,1536]{1,0:T(8,128)(2,1)}) %all-gather.14.cloned.1.call-update) | async-done | bytes 1572880 | tf_op jit(solution)/shard_map/all_gather | solution.py:90
  88.0 79.3 %all-gather.8.cloned.1.call-done = bf16[1536,2,384]{2,1,0:T(2,128)(2,1)} async-done(((bf16[24,2,384]{2,1,0:T(2,128)(2,1)}), bf16[1536,2,384]{2,1,0:T(2,128)(2,1)}) %all-gather.8.cloned.1.call-update) | async-done | bytes 2359312 | tf_op jit(solution)/shard_map/all_gather | solution.py:98
  174.2 70.2 %all-gather.10.cloned.1.call-done = bf16[384,1536]{0,1:T(8,128)(2,1)} async-done(((bf16[384,24]{0,1:T(8,128)(2,1)}), bf16[384,1536]{0,1:T(8,128)(2,1)}) %all-gather.10.cloned.1.call-update) | async-done | bytes 1179664 | tf_op jit(solution)/shard_map/all_gather | solution.py:99
  244.4 27.2 %all-gather.12.cloned.1.call-done = bf16[512,1536]{1,0:T(8,128)(2,1)} async-done(((bf16[512,384]{1,0:T(8,128)(2,1)}), bf16[512,1536]{1,0:T(8,128)(2,1)}) %all-gather.12.cloned.1.call-update) | async-done | bytes 1572880 | tf_op jit(solution)/shard_map/all_gather | solution.py:114
  271.6 8.2 multiply_reduce_fusion.1
  281.6 3.8 fusion.12
  285.4 8.2 copy.19
  294.2 2.6 convolution_convert_fusion.1
  298.5 4.4 convolution_convert_fusion
  303.3 3.9 fusion.46
  310.6 181.5 %all-reduce.20.cloned.1.call-done = f32[1536,2,384]{2,1,0:T(2,128)} async-done(((f32[1536,2,384]{2,1,0:T(2,128)}), f32[1536,2,384]{2,1,0:T(2,128)}) %all-reduce.20.cloned.1.call-update) | async-done | bytes 4718608
  493.6 26.4 %reduce-scatter.7.cloned.1.call-done = bf16[384,512]{1,0:T(8,128)(2,1)} async-done(((bf16[1536,512]{1,0:T(8,128)(2,1)}), bf16[384,512]{1,0:T(8,128)(2,1)}) %reduce-scatter.7.cloned.1.call-update) | async-done | bytes 393232
  521.2 69.5 %all-gather.16.cloned.1.call-done = bf16[2048,1536]{1,0:T(8,128)(2,1)} async-done(((bf16[512,1536]{1,0:T(8,128)(2,1)}), bf16[2048,1536]{1,0:T(8,128)(2,1)}) %all-gather.16.cloned.1.call-update) | async-done | bytes 6291472 | tf_op jit(solution)/shard_map/all_gather | solution.py:146
  590.7 4.7 reduce_sum.150
  600.3 10.5 %all-to-all-start.2 = ((bf16[64,8,384]{2,1,0:T(8,128)(2,1)}), bf16[64,8,384]{2,1,0:T(8,128)(2,1)S(1)}, u32[]{:S(2)}, u32[]{:S(2)}) async-start(bf16[64,8,384]{2,1,0:T(8,128)(2,1)} %bitcast.8), calls=%async_computation.2 | async-start | bytes 786432 | tf_op jit(solution)/shard_map/all_to_all | solution.py:160
  611.6 119.0 %reduce-scatter.9.cloned.1.call-done = f32[384,24]{0,1:T(8,128)} async-done(((f32[384,1536]{0,1:T(8,128)}), f32[384,24]{0,1:T(8,128)}) %reduce-scatter.9.cloned.1.call-update) | async-done | bytes 36880
  732.0 246.1 %all-reduce.17 = (f32[384]{0:T(512)S(1)}, f32[9,384]{1,0:T(8,128)S(1)}) all-reduce(f32[384]{0:T(512)S(1)} %get-tuple-element.30, f32[9,384]{1,0:T(8,128)S(1)} %copy-done.8), channel_id=1, replica_groups=mesh['dp'=64,'seq'=4] {'dp'}, use_global_device_ids=true, to_apply=%region_12.13 | all-reduce | flops 3840 | bytes 30720 | tf_op jit(solution)/shard_map/psum | solution.py:156
  979.4 2.6 gather_fusion.4
  (144 shorter events, 43.2 us)
Async XLA Ops:
  7.2 22.1 %copy-start.6 = (bf16[512,384]{1,0:T(8,128)(2,1)S(1)}, bf16[512,384]{1,0:T(8,128)(2,1)}, u32[]{:S(2)}) copy-start(bf16[512,384]{1,0:T(8,128)(2,1)} %param.8) | copy-start | bytes 1179652
  10.9 3.2 copy-start.11
  17.1 21.6 %all-to-all-start.1 = ((s32[64,1,8]{2,1,0:T(1,128)}), s32[64,1,8]{2,1,0:T(1,128)S(1)}, u32[]{:S(2)}, u32[]{:S(2)}) async-start(s32[64,1,8]{2,1,0:T(1,128)} %bitcast.4), calls=%async_computation.1 | async-start | bytes 65536 | tf_op jit(solution)/shard_map/all_to_all | solution.py:87
  38.7 19.1 %all-to-all-start = ((bf16[64,8,384]{2,1,0:T(8,128)(2,1)}), bf16[64,8,384]{2,1,0:T(8,128)(2,1)S(1)}, u32[]{:S(2)}, u32[]{:S(2)}) async-start(bf16[64,8,384]{2,1,0:T(8,128)(2,1)} %bitcast.2), calls=%async_computation | async-start | bytes 786432 | tf_op jit(solution)/shard_map/all_to_all | solution.py:86
  43.3 42.2 %all-gather.14.cloned.1.call-start = ((), (), s32[]{:S(2)}) async-start(), calls=%async_computation.8 | async-start | bytes 1966080 | tf_op jit(solution)/shard_map/all_gather | solution.py:90
  44.7 13.1 %copy-start.13 = (s32[512,1]{0,1:T(1,128)}, s32[512,1]{0,1:T(1,128)S(1)}, u32[]{:S(2)}) copy-start(s32[512,1]{0,1:T(1,128)S(1)} %compare_select_fusion) | copy-start | bytes 6148
  57.9 4.9 copy-start.15
  57.9 5.0 copy-start.16
  60.5 106.8 %all-gather.8.cloned.1.call-start = ((), (), s32[]{:S(2)}) async-start(), calls=%async_computation.5 | async-start | bytes 2396160 | tf_op jit(solution)/shard_map/all_gather | solution.py:98
  61.3 183.1 %all-gather.10.cloned.1.call-start = ((), (), s32[]{:S(2)}) async-start(), calls=%async_computation.6 | async-start | bytes 1198080 | tf_op jit(solution)/shard_map/all_gather | solution.py:99
  62.0 209.6 %all-gather.12.cloned.1.call-start = ((), (), s32[]{:S(2)}) async-start(), calls=%async_computation.7 | async-start | bytes 1966080 | tf_op jit(solution)/shard_map/all_gather | solution.py:114
  62.6 429.5 %all-reduce.20.cloned.1.call-start = ((), (), s32[]{:S(2)}) async-start(), calls=%async_computation.11 | async-start | bytes 9437184
  63.0 208.7 %copy-start.26 = (f32[512]{0:T(512)}, f32[512]{0:T(512)S(1)}, u32[]{:S(2)}) copy-start(f32[512]{0:T(512)S(1)} %compare_convert_fusion) | copy-start | bytes 6148
  167.3 2.2 copy-start.9
  281.6 3.8 copy-start.7
  293.6 226.4 %reduce-scatter.7.cloned.1.call-start = ((), (), s32[]{:S(2)}) async-start(), calls=%async_computation.10 | async-start | bytes 1966080
  298.5 4.8 copy-start.5
  298.5 292.3 %all-gather.16.cloned.1.call-start = ((), (), s32[]{:S(2)}) async-start(), calls=%async_computation.9 | async-start | bytes 7864320 | tf_op jit(solution)/shard_map/all_gather | solution.py:146
  303.0 427.6 %reduce-scatter.9.cloned.1.call-start = ((), (), s32[]{:S(2)}) async-start(), calls=%async_computation.12 | async-start | bytes 2396160
  307.3 2.0 copy-start.18
  307.3 2.0 copy-start.17
  597.7 13.1 %copy-start.1 = (bf16[512,384]{1,0:T(8,128)(2,1)S(1)}, bf16[512,384]{1,0:T(8,128)(2,1)}, u32[]{:S(2)}) copy-start(bf16[512,384]{1,0:T(8,128)(2,1)} %gather_fusion.2) | copy-start | bytes 1179652
  597.7 134.3 %copy-start.8 = (f32[9,384]{1,0:T(8,128)S(1)}, f32[9,384]{1,0:T(8,128)}, u32[]{:S(2)}) copy-start(f32[9,384]{1,0:T(8,128)} %stack.39) | copy-start | bytes 41476
  600.3 379.1 %all-to-all-start.2 = ((bf16[64,8,384]{2,1,0:T(8,128)(2,1)}), bf16[64,8,384]{2,1,0:T(8,128)(2,1)S(1)}, u32[]{:S(2)}, u32[]{:S(2)}) async-start(bf16[64,8,384]{2,1,0:T(8,128)(2,1)} %bitcast.8), calls=%async_computation.2 | async-start | bytes 786432 | tf_op jit(solution)/shard_map/all_to_all | solution.py:160
  (16 other events, 25.2 us)
Sparse Core Ops, SparseCore 0:
  60.6 24.8 all-gather.13
  88.2 79.0 all-gather.7
  170.0 74.3 all-gather.9
  246.1 25.4 all-gather.11
  293.7 198.3 all-reduce.19
  494.5 25.4 reduce-scatter.6
  521.8 68.8 all-gather.15
  594.9 135.6 reduce-scatter.8
